TPU v7x, 512 devices: a whole 4x8x8 slice. The times are simulated.
512 devices in a mesh: dom: 128 (over z, y, core), feat: 4 (over x).
Axes of the slice: x: 4, y: 8, z: 8, core: 2. Of those that a mesh axis runs over, the one named last changes fastest.
Arguments:
- node_feats: bfloat16 [256, 262144], P('feat', 'dom'), may hold values from -6 to 6
- weight: bfloat16 [256, 256], P(None, 'feat'), may hold values from -0.375 to 0.375
- bias_vec: bfloat16 [256], P('feat'), may hold values from -3 to 3
- adj_tiles: bfloat16 [12288, 128, 128], P('dom'), may hold values from -0.25 to 0.25
- tile_row: int32 [12288], P('dom'), may hold values from 0 to 15, as said below
- tile_col: int32 [12288], P('dom'), may hold values from 0 to 143, as said below
- tile_count: int32 [128], P('dom'), may hold values from 58 to 96
- send_block: int32 [16384], P('dom'), may hold values from 0 to 15, as said below
- cotangent: bfloat16 [256, 262144], P('feat', 'dom'), may hold values from -6 to 6
Outputs:
- activations: bfloat16 [256, 262144], P('feat', 'dom')
- grad_input: bfloat16 [256, 262144], P('feat', 'dom')
- grad_weight: float32 [256, 256], P(None, 'feat')
- grad_bias: float32 [256], P('feat')
Inputs may be any that keep to these rules, and one draw needn't show every extreme that they name: `tile_row`: entries past a partition's tile_count are padding, of the same range. `tile_col`: among a partition's valid entries, each peer's halo slot 16 + q is named at most once, and a partition's own slot never. `send_block`: entry q * 128 + p is the local block that partition q sends to partition p; it is defined for every pair.
All inputs are finite; a program needn't handle non-finite values.
Results may differ from a plain program's by a relative error of at most 0.0064.
Values may be sent and summed in bfloat16 or wider, within the bound.
No kernel may reach another device: no remote copies, remote signals or barrier semaphores. Data moves between devices by JAX's collectives and lax.ppermute only.
A program may use at most 64 MiB of HBM per device.

v0:
```python
import math
import jax
import jax.numpy as jnp
from jax import lax
from jax.sharding import PartitionSpec as P


def smooth_gate(values):
    return jax.nn.gelu(values, approximate=True)


def per_device(
    node_feats, weight, bias_vec, adj_tiles, tile_row, tile_col, tile_count, send_block, cotangent
):
    feat_rows, node_rows = node_feats.shape
    tile_slots = adj_tiles.shape[0]
    tile_size = adj_tiles.shape[1]
    blocks = node_rows // tile_size
    domains = lax.axis_size("dom")
    whole = lax.all_gather(node_feats, "feat", axis=0, tiled=True)
    hidden = lax.dot_general(
        weight, whole, (((0,), (0,)), ((), ())), preferred_element_type=jnp.float32
    ).astype(jnp.bfloat16)
    hid_blocks = hidden.reshape(feat_rows, blocks, tile_size)
    outgoing = jnp.take(hid_blocks, send_block, axis=1)
    incoming = lax.all_to_all(outgoing, "dom", split_axis=1, concat_axis=1, tiled=True)
    sources = jnp.concatenate([hid_blocks, incoming], axis=1)
    live_tiles = jnp.arange(tile_slots) < tile_count[0]
    live_float = live_tiles.astype(jnp.float32)
    row_place = (tile_row[:, None] == jnp.arange(blocks)[None, :]).astype(jnp.float32) * live_float[
        :, None
    ]
    picked = jnp.take(sources, tile_col, axis=1)
    products = jnp.einsum("otb,tab->ota", picked, adj_tiles, preferred_element_type=jnp.float32)
    summed = jnp.einsum(
        "ota,tr->ora", products, row_place, precision=lax.Precision.HIGHEST
    ).reshape(feat_rows, node_rows)
    preact = summed + bias_vec.astype(jnp.float32)[:, None]
    activated, pullback = jax.vjp(smooth_gate, preact)
    grad_pre = pullback(cotangent.astype(jnp.float32))[0]
    grad_low = grad_pre.astype(jnp.bfloat16)
    grad_blocks = grad_low.reshape(feat_rows, blocks, tile_size)
    rows_picked = jnp.take(grad_blocks, tile_row, axis=1)
    backward = jnp.einsum(
        "ota,tab->otb", rows_picked, adj_tiles, preferred_element_type=jnp.float32
    )
    src_place = (tile_col[:, None] == jnp.arange(blocks + domains)[None, :]).astype(
        jnp.float32
    ) * live_float[:, None]
    recv_place = (send_block[:, None] == jnp.arange(blocks)[None, :]).astype(jnp.float32)
    own_sum = jnp.einsum(
        "otb,tr->orb", backward, src_place[:, :blocks], precision=lax.Precision.HIGHEST
    )
    slot_hit = jnp.logical_and(
        tile_col[:, None] == blocks + jnp.arange(domains)[None, :], live_tiles[:, None]
    )
    slot_rows = jnp.sum(jnp.where(slot_hit, tile_row[:, None], 0), axis=0)
    out_tiles = jnp.einsum(
        "tq,tab->qab", slot_hit.astype(jnp.bfloat16), adj_tiles, preferred_element_type=jnp.float32
    ).astype(jnp.bfloat16)
    out_rows = jnp.take(grad_blocks, slot_rows, axis=1)
    in_tiles = lax.all_to_all(out_tiles, "dom", split_axis=0, concat_axis=0, tiled=True)
    in_rows = lax.all_to_all(out_rows, "dom", split_axis=1, concat_axis=1, tiled=True)
    remote_sum = jnp.einsum("oqa,qab->oqb", in_rows, in_tiles, preferred_element_type=jnp.float32)
    grad_sum = own_sum + jnp.einsum(
        "oqb,qr->orb", remote_sum, recv_place, precision=lax.Precision.HIGHEST
    )
    grad_hidden = grad_sum.reshape(feat_rows, node_rows).astype(jnp.bfloat16)
    norm_scale = 1.0 / math.sqrt(domains * node_rows)
    weight_part = lax.dot_general(
        whole, grad_hidden, (((1,), (1,)), ((), ())), preferred_element_type=jnp.float32
    )
    bias_part = jnp.sum(grad_pre, axis=1)
    weight_sum, bias_sum = lax.psum((weight_part, bias_part), "dom")
    grad_weight = weight_sum * norm_scale
    grad_bias = bias_sum * norm_scale
    full_weight, all_grad = (
        lax.all_gather(weight, "feat", axis=1, tiled=True),
        lax.all_gather(grad_hidden, "feat", axis=0, tiled=True),
    )
    my_rows = lax.dynamic_slice_in_dim(
        full_weight, lax.axis_index("feat") * feat_rows, feat_rows, 0
    )
    grad_input = jnp.dot(my_rows, all_grad, preferred_element_type=jnp.float32).astype(jnp.bfloat16)
    return (activated.astype(jnp.bfloat16), grad_input, grad_weight, grad_bias)


def solution(mesh):
    placed = (
        P("feat", "dom"),
        P(None, "feat"),
        P("feat"),
        P("dom", None, None),
        P("dom"),
        P("dom"),
        P("dom"),
        P("dom"),
        P("feat", "dom"),
    )
    return jax.shard_map(
        per_device,
        mesh=mesh,
        in_specs=placed,
        out_specs=(P("feat", "dom"), P("feat", "dom"), P(None, "feat"), P("feat")),
        check_vma=False,
    )
```

profile of v0, /device:TPU:1, one launch (start us, length us, event | category | flops | bytes accessed | tf_op | source)
XLA Modules:
  0.0 581.7 jit_solution(17211733674106753430)
XLA Ops:
  7.2 0.7 all-gather.3.cloned.1.call-update
  7.9 0.9 compare_select_fusion.1
  9.4 34.6 %all-gather.3.cloned.1.call-done = bf16[256,2048]{1,0:T(8,128)(2,1)} async-done(((bf16[64,2048]{1,0:T(8,128)(2,1)}), bf16[256,2048]{1,0:T(8,128)(2,1)}) %all-gather.3.cloned.1.call-update) | async-done | bytes 1048592 | tf_op jit(solution)/shard_map/all_gather | solution.py:20
  44.0 1.5 fusion.23
  45.6 2.2 gather_fusion.2
  47.8 3.2 select_bitcast_fusion.1
  51.0 15.8 %all-to-all-start = ((bf16[64,128,128]{2,0,1:T(8,128)(2,1)}), bf16[64,128,128]{2,0,1:T(8,128)(2,1)}, u32[]{:S(2)}, u32[]{:S(2)}) async-start(bf16[64,128,128]{2,0,1:T(8,128)(2,1)} %select_bitcast_fusion.1), calls=%async_computation | async-start | bytes 4194304 | tf_op jit(solution)/shard_map/all_to_all | solution.py:26
  67.5 2.9 fusion.8
  70.4 4.7 copy.30
  75.1 42.6 %all-to-all-done = bf16[64,128,128]{2,0,1:T(8,128)(2,1)} async-done(((bf16[64,128,128]{2,0,1:T(8,128)(2,1)}), bf16[64,128,128]{2,0,1:T(8,128)(2,1)}, u32[]{:S(2)}, u32[]{:S(2)}) %all-to-all-start) | async-done | bytes 2097184 | tf_op jit(solution)/shard_map/all_to_all | solution.py:26
  117.7 9.3 %all-to-all-start.1 = ((bf16[128,128,128]{2,1,0:T(8,128)(2,1)}), bf16[128,128,128]{2,1,0:T(8,128)(2,1)}, u32[]{:S(2)}, u32[]{:S(2)}) async-start(bf16[128,128,128]{2,1,0:T(8,128)(2,1)} %copy.30), calls=%async_computation.1 | async-start | bytes 8388608 | tf_op jit(solution)/shard_map/all_to_all | solution.py:62
  127.3 3.3 pad_maximum_fusion
  130.6 3.6 gather_fusion
  134.2 3.6 convolution_bitcast_fusion.2
  137.8 3.3 fusion.6
  141.1 1.3 fusion.61
  142.6 2.1 gather_fusion.3
  144.7 3.2 select_bitcast_fusion
  147.9 75.7 %all-to-all-done.1 = bf16[128,128,128]{2,1,0:T(8,128)(2,1)} async-done(((bf16[128,128,128]{2,1,0:T(8,128)(2,1)}), bf16[128,128,128]{2,1,0:T(8,128)(2,1)}, u32[]{:S(2)}, u32[]{:S(2)}) %all-to-all-start.1) | async-done | bytes 4194336 | tf_op jit(solution)/shard_map/all_to_all | solution.py:62
  223.6 22.7 %all-to-all-start.2 = ((bf16[64,128,128]{2,0,1:T(8,128)(2,1)}), bf16[64,128,128]{2,0,1:T(8,128)(2,1)}, u32[]{:S(2)}, u32[]{:S(2)}) async-start(bf16[64,128,128]{2,0,1:T(8,128)(2,1)} %select_bitcast_fusion), calls=%async_computation.2 | async-start | bytes 4194304 | tf_op jit(solution)/shard_map/all_to_all | solution.py:63
  246.6 2.0 gather_fusion.1
  248.6 4.1 convolution_bitcast_fusion.1
  252.7 44.5 %all-to-all-done.2 = bf16[64,128,128]{2,0,1:T(8,128)(2,1)} async-done(((bf16[64,128,128]{2,0,1:T(8,128)(2,1)}), bf16[64,128,128]{2,0,1:T(8,128)(2,1)}, u32[]{:S(2)}, u32[]{:S(2)}) %all-to-all-start.2) | async-done | bytes 2097184 | tf_op jit(solution)/shard_map/all_to_all | solution.py:63
  297.2 4.0 convolution_bitcast_fusion
  301.3 3.8 fusion
  305.2 3.3 fusion.20
  308.5 1.1 convolution_bitcast_fusion.3
  309.6 0.8 copy.67
  310.4 9.1 %all_gather.10 = bf16[256,256]{0,1:T(8,128)(2,1)S(1)} all-gather(bf16[256,64]{0,1:T(8,128)(2,1)S(1)} %copy-done.4), channel_id=1, replica_groups=mesh['dom'=128,'feat'=4] {'feat'}, dimensions={1}, use_global_device_ids=true | all-gather | bytes 163840 | tf_op jit(solution)/shard_map/all_gather | solution.py:78
  319.5 251.3 %psum.15 = f32[64]{0:T(128)S(1)} all-reduce(f32[64]{0:T(128)S(1)} %get-tuple-element.5), channel_id=1, replica_groups=mesh['dom'=128,'feat'=4] {'dom'}, use_global_device_ids=true, to_apply=%region_3.5 | all-reduce | flops 64 | bytes 512 | tf_op jit(solution)/shard_map/psum | solution.py:74
  571.3 1.5 broadcast_multiply_fusion
  572.8 2.3 convolution_convert_fusion
  (44 shorter events, 1.9 us)
Async XLA Ops:
  7.2 60.3 %copy-start = (bf16[96,128,128]{2,1,0:T(8,128)(2,1)S(1)}, bf16[96,128,128]{2,1,0:T(8,128)(2,1)}, u32[]{:S(2)}) copy-start(bf16[96,128,128]{2,1,0:T(8,128)(2,1)} %param.14) | copy-start | bytes 9437188
  7.2 36.8 %all-gather.3.cloned.1.call-start = ((), (), s32[]{:S(2)}) async-start(), calls=%async_computation.3 | async-start | bytes 1310720 | tf_op jit(solution)/shard_map/all_gather | solution.py:20
  51.0 16.5 %copy-start.5 = (s32[96]{0:T(128)S(1)}, s32[96]{0:T(128)}, u32[]{:S(2)}) copy-start(s32[96]{0:T(128)} %param.16) | copy-start | bytes 1156
  51.0 66.7 %all-to-all-start = ((bf16[64,128,128]{2,0,1:T(8,128)(2,1)}), bf16[64,128,128]{2,0,1:T(8,128)(2,1)}, u32[]{:S(2)}, u32[]{:S(2)}) async-start(bf16[64,128,128]{2,0,1:T(8,128)(2,1)} %select_bitcast_fusion.1), calls=%async_computation | async-start | bytes 4194304 | tf_op jit(solution)/shard_map/all_to_all | solution.py:26
  75.1 52.0 %copy-start.8 = (bf16[64]{0:T(256)(128)(2,1)S(1)}, bf16[64]{0:T(256)(128)(2,1)}, u32[]{:S(2)}) copy-start(bf16[64]{0:T(256)(128)(2,1)} %param.13) | copy-start | bytes 388
  75.1 52.0 %copy-start.6 = (s32[96]{0:T(128)S(1)}, s32[96]{0:T(128)}, u32[]{:S(2)}) copy-start(s32[96]{0:T(128)} %param.15) | copy-start | bytes 1156
  117.7 105.8 %all-to-all-start.1 = ((bf16[128,128,128]{2,1,0:T(8,128)(2,1)}), bf16[128,128,128]{2,1,0:T(8,128)(2,1)}, u32[]{:S(2)}, u32[]{:S(2)}) async-start(bf16[128,128,128]{2,1,0:T(8,128)(2,1)} %copy.30), calls=%async_computation.1 | async-start | bytes 8388608 | tf_op jit(solution)/shard_map/all_to_all | solution.py:62
  137.8 3.3 copy-start.3
  223.6 73.6 %all-to-all-start.2 = ((bf16[64,128,128]{2,0,1:T(8,128)(2,1)}), bf16[64,128,128]{2,0,1:T(8,128)(2,1)}, u32[]{:S(2)}, u32[]{:S(2)}) async-start(bf16[64,128,128]{2,0,1:T(8,128)(2,1)} %select_bitcast_fusion), calls=%async_computation.2 | async-start | bytes 4194304 | tf_op jit(solution)/shard_map/all_to_all | solution.py:63
  246.3 325.0 %all-reduce.2.cloned.1.call-start = ((), (), s32[]{:S(2)}) async-start(), calls=%async_computation.5 | async-start | bytes 131072 | tf_op jit(solution)/shard_map/psum | solution.py:74
  252.7 48.5 %copy-start.7 = (s32[128]{0:T(128)S(1)}, s32[128]{0:T(128)}, u32[]{:S(2)}) copy-start(s32[128]{0:T(128)} %param.18) | copy-start | bytes 1540
  301.3 3.9 copy-start.1
  305.1 3.3 copy-start.2
  305.1 5.3 copy-start.4
  309.6 263.2 %all-gather.5.cloned.1.call-start = ((), (), s32[]{:S(2)}) async-start(), calls=%async_computation.4 | async-start | bytes 1310720 | tf_op jit(solution)/shard_map/all_gather | solution.py:79
Sparse Core Ops, SparseCore 0:
  10.1 33.8 all-gather.2
  309.7 175.5 all-reduce.1
  488.0 21.2 all-gather.4
where the time goes:
time: 582 us
  blocking collectives  260 us (45%)
  waiting for transfers between devices  198 us (34%)
  starting transfers between devices  48.1 us (8%)
  matrix products  30.1 us (5%)
  local copies, waits for them, and re-layouts  15.6 us (3%)
  other arithmetic  14.7 us (3%)
  between operations  14.7 us (3%)
    psum x1, blocking collectives, per_device(): weight_sum, bias_sum = lax.psum((weight_part, bias_part), 'dom')  251 us
    all_to_all x1, waiting for transfers between devices, per_device(): lax.all_to_all(out_tiles, 'dom', split_axis=0, concat_axis=0, tiled=True)  75.7 us
    all_to_all x1, waiting for transfers between devices, per_device(): lax.all_to_all(out_rows, 'dom', split_axis=1, concat_axis=1, tiled=True)  44.5 us
    all_to_all x1, waiting for transfers between devices, per_device(): lax.all_to_all(outgoing, 'dom', split_axis=1, concat_axis=1, tiled=True)  42.6 us
    all_gather x1, waiting for transfers between devices, per_device(): whole = lax.all_gather(node_feats, 'feat', axis=0, tiled=True)  34.6 us
    all_to_all x1, starting transfers between devices, per_device(): lax.all_to_all(out_rows, 'dom', split_axis=1, concat_axis=1, tiled=True)  22.7 us
    all_to_all x1, starting transfers between devices, per_device(): lax.all_to_all(outgoing, 'dom', split_axis=1, concat_axis=1, tiled=True)  15.8 us
  transfers between devices with their start and end apart: 6, of which 4 were waited for; matrix products, arithmetic and copies ran while one was open for 7% of the time, Pallas kernels for 0%

commit v1 on v0

--- a/solution.py
+++ b/solution.py
@@ -3,6 +3,18 @@
 import jax.numpy as jnp
 from jax import lax
 from jax.sharding import PartitionSpec as P
+
+
+def _watch_rows(device_axis, field_in):
+    degree = lax.axis_size(device_axis)
+    left_arr = [(b - 1, b) for b in range(1, degree)] + [(degree - 1, 0)]
+    built = field_in
+    made = [built]
+    for _ in range(degree - 1):
+        built = lax.ppermute(built, axis_name=device_axis, perm=left_arr)
+        made += [built]
+    now = jnp.concatenate([*reversed(made)], axis=0)
+    return jnp.roll(now, (lax.axis_index(device_axis) + 1) * built.shape[0], axis=0)
 
 
 def smooth_gate(values):
@@ -17,7 +29,7 @@
     tile_size = adj_tiles.shape[1]
     blocks = node_rows // tile_size
     domains = lax.axis_size("dom")
-    whole = lax.all_gather(node_feats, "feat", axis=0, tiled=True)
+    whole = _watch_rows("feat", node_feats)
     hidden = lax.dot_general(
         weight, whole, (((0,), (0,)), ((), ())), preferred_element_type=jnp.float32
     ).astype(jnp.bfloat16)

time: 582 us -> 589 us (1.012)
  waiting for transfers between devices: 198 us -> 181 us
  starting transfers between devices: 48.1 us -> 63.9 us
  local copies, waits for them, and re-layouts: 15.6 us -> 23.5 us
    all_gather x1 -> x0, waiting for transfers between devices: 34.6 us -> none  [per_device(): whole = lax.all_gather(node_feats, 'feat', axis=0, tiled=True)]
    ppermute x0 -> x3, waiting for transfers between devices: none -> 17.8 us  [_watch_rows(): built = lax.ppermute(built, axis_name=device_axis, perm=left_arr)]
    ppermute x0 -> x3, starting transfers between devices: none -> 9.28 us  [_watch_rows(): built = lax.ppermute(built, axis_name=device_axis, perm=left_arr)]
    unnamed x19 -> x34, local copies, waits for them, and re-layouts: 0.82 us -> 8.7 us
    all_to_all x1, starting transfers between devices: 15.8 us -> 22.3 us  [per_device(): lax.all_to_all(outgoing, 'dom', split_axis=1, concat_axis=1, tiled=True)]
  transfers between devices with their start and end apart: 6 -> 8, of which waited for: 4 -> 6; matrix products, arithmetic and copies ran while one was open for 7% -> 7% of each run, Pallas kernels for 0% -> 0%
where the time goes in v1:
time: 589 us; the launch traced here: 588 us
  blocking collectives  260 us (44%)
  waiting for transfers between devices  181 us (31%)
  starting transfers between devices  63.9 us (11%)
  matrix products  28.8 us (5%)
  local copies, waits for them, and re-layouts  23.5 us (4%)
  between operations  16.5 us (3%)
  other arithmetic  14.5 us (2%)
    psum x1, blocking collectives, per_device(): weight_sum, bias_sum = lax.psum((weight_part, bias_part), 'dom')  251 us
    all_to_all x1, waiting for transfers between devices, per_device(): lax.all_to_all(out_tiles, 'dom', split_axis=0, concat_axis=0, tiled=True)  75.8 us
    all_to_all x1, waiting for transfers between devices, per_device(): lax.all_to_all(out_rows, 'dom', split_axis=1, concat_axis=1, tiled=True)  44.5 us
    all_to_all x1, waiting for transfers between devices, per_device(): lax.all_to_all(outgoing, 'dom', split_axis=1, concat_axis=1, tiled=True)  42.6 us
    all_to_all x1, starting transfers between devices, per_device(): lax.all_to_all(out_rows, 'dom', split_axis=1, concat_axis=1, tiled=True)  22.7 us
    all_to_all x1, starting transfers between devices, per_device(): lax.all_to_all(outgoing, 'dom', split_axis=1, concat_axis=1, tiled=True)  22.3 us
    ppermute x3, waiting for transfers between devices, _watch_rows(): built = lax.ppermute(built, axis_name=device_axis, perm=left_arr)  17.8 us
  transfers between devices with their start and end apart: 8, of which 6 were waited for; matrix products, arithmetic and copies ran while one was open for 7% of the time, Pallas kernels for 0%

profile of v1, /device:TPU:1, one launch (start us, length us, event | category | flops | bytes accessed | tf_op | source)
XLA Modules:
  0.0 588.2 jit_solution(17329568482436748333)
XLA Ops:
  8.0 4.2 collective-permute-start
  12.2 5.2 collective-permute-done
  18.2 3.2 collective-permute-start.1
  22.0 5.3 collective-permute-done.1
  27.3 1.9 collective-permute-start.2
  30.0 7.2 %collective-permute-done.2 = bf16[64,2048]{1,0:T(8,128)(2,1)} collective-permute-done((bf16[64,2048]{1,0:T(8,128)(2,1)}, bf16[64,2048]{1,0:T(8,128)(2,1)}, u32[]{:S(2)}, u32[]{:S(2)}) %collective-permute-start.2) | collective-permute-done | bytes 262176 | tf_op jit(solution)/shard_map/ppermute | solution.py:14
  44.9 2.1 gather_fusion.2
  47.0 3.2 select_bitcast_fusion.1
  50.2 22.3 %all-to-all-start = ((bf16[64,128,128]{2,0,1:T(8,128)(2,1)}), bf16[64,128,128]{2,0,1:T(8,128)(2,1)}, u32[]{:S(2)}, u32[]{:S(2)}) async-start(bf16[64,128,128]{2,0,1:T(8,128)(2,1)} %select_bitcast_fusion.1), calls=%async_computation | async-start | bytes 4194304 | tf_op jit(solution)/shard_map/all_to_all | solution.py:38
  73.2 2.9 fusion.8
  76.1 4.7 copy.30
  80.8 42.6 %all-to-all-done = bf16[64,128,128]{2,0,1:T(8,128)(2,1)} async-done(((bf16[64,128,128]{2,0,1:T(8,128)(2,1)}), bf16[64,128,128]{2,0,1:T(8,128)(2,1)}, u32[]{:S(2)}, u32[]{:S(2)}) %all-to-all-start) | async-done | bytes 2097184 | tf_op jit(solution)/shard_map/all_to_all | solution.py:38
  123.4 9.3 %all-to-all-start.1 = ((bf16[128,128,128]{2,1,0:T(8,128)(2,1)}), bf16[128,128,128]{2,1,0:T(8,128)(2,1)}, u32[]{:S(2)}, u32[]{:S(2)}) async-start(bf16[128,128,128]{2,1,0:T(8,128)(2,1)} %copy.30), calls=%async_computation.1 | async-start | bytes 8388608 | tf_op jit(solution)/shard_map/all_to_all | solution.py:74
  133.0 3.2 pad_maximum_fusion
  136.2 3.6 gather_fusion
  139.8 3.6 convolution_bitcast_fusion.2
  143.4 3.3 fusion.6
  146.7 1.3 fusion.65
  148.1 2.1 gather_fusion.3
  150.3 3.2 select_bitcast_fusion
  153.5 75.8 %all-to-all-done.1 = bf16[128,128,128]{2,1,0:T(8,128)(2,1)} async-done(((bf16[128,128,128]{2,1,0:T(8,128)(2,1)}), bf16[128,128,128]{2,1,0:T(8,128)(2,1)}, u32[]{:S(2)}, u32[]{:S(2)}) %all-to-all-start.1) | async-done | bytes 4194336 | tf_op jit(solution)/shard_map/all_to_all | solution.py:74
  229.2 22.7 %all-to-all-start.2 = ((bf16[64,128,128]{2,0,1:T(8,128)(2,1)}), bf16[64,128,128]{2,0,1:T(8,128)(2,1)}, u32[]{:S(2)}, u32[]{:S(2)}) async-start(bf16[64,128,128]{2,0,1:T(8,128)(2,1)} %select_bitcast_fusion), calls=%async_computation.2 | async-start | bytes 4194304 | tf_op jit(solution)/shard_map/all_to_all | solution.py:75
  252.3 2.0 gather_fusion.1
  254.3 4.1 convolution_bitcast_fusion.1
  258.4 44.5 %all-to-all-done.2 = bf16[64,128,128]{2,0,1:T(8,128)(2,1)} async-done(((bf16[64,128,128]{2,0,1:T(8,128)(2,1)}), bf16[64,128,128]{2,0,1:T(8,128)(2,1)}, u32[]{:S(2)}, u32[]{:S(2)}) %all-to-all-start.2) | async-done | bytes 2097184 | tf_op jit(solution)/shard_map/all_to_all | solution.py:75
  302.9 4.0 convolution_bitcast_fusion
  306.9 3.8 fusion
  310.8 3.3 fusion.20
  316.1 9.1 %all_gather.6 = bf16[256,256]{0,1:T(8,128)(2,1)S(1)} all-gather(bf16[256,64]{0,1:T(8,128)(2,1)S(1)} %copy-done.8), channel_id=1, replica_groups=mesh['dom'=128,'feat'=4] {'feat'}, dimensions={1}, use_global_device_ids=true | all-gather | bytes 163840 | tf_op jit(solution)/shard_map/all_gather | solution.py:90
  325.2 251.3 %psum.15 = f32[64]{0:T(128)S(1)} all-reduce(f32[64]{0:T(128)S(1)} %get-tuple-element.5), channel_id=1, replica_groups=mesh['dom'=128,'feat'=4] {'dom'}, use_global_device_ids=true, to_apply=%region_3.5 | all-reduce | flops 64 | bytes 512 | tf_op jit(solution)/shard_map/psum | solution.py:86
  577.0 1.5 broadcast_multiply_fusion
  578.4 2.3 convolution_convert_fusion.1
  (63 shorter events, 12.7 us)
Async XLA Ops:
  8.0 65.2 %copy-start = (bf16[96,128,128]{2,1,0:T(8,128)(2,1)S(1)}, bf16[96,128,128]{2,1,0:T(8,128)(2,1)}, u32[]{:S(2)}) copy-start(bf16[96,128,128]{2,1,0:T(8,128)(2,1)} %param.14) | copy-start | bytes 9437188
  8.0 35.1 %copy-start.4 = (bf16[64,2048]{1,0:T(8,128)(2,1)S(1)}, bf16[64,2048]{1,0:T(8,128)(2,1)}, u32[]{:S(2)}) copy-start(bf16[64,2048]{1,0:T(8,128)(2,1)} %param.11) | copy-start | bytes 786436
  8.0 9.4 %collective-permute-start = (bf16[64,2048]{1,0:T(8,128)(2,1)}, bf16[64,2048]{1,0:T(8,128)(2,1)S(1)}, u32[]{:S(2)}, u32[]{:S(2)}) collective-permute-start(bf16[64,2048]{1,0:T(8,128)(2,1)} %param.11), channel_id=1, source_target_pairs={{0,1},{1,2},{2,3},{3,0},{4,5},{5,6},{6,7},{7,4},{8,9},{9,10},{10,1... | collective-permute-start | bytes 786440 | tf_op jit(solution)/shard_map/ppermute | solution.py:14
  17.5 0.7 copy-start.5
  18.2 9.2 %collective-permute-start.1 = (bf16[64,2048]{1,0:T(8,128)(2,1)S(1)}, bf16[64,2048]{1,0:T(8,128)(2,1)}, u32[]{:S(2)}, u32[]{:S(2)}) collective-permute-start(bf16[64,2048]{1,0:T(8,128)(2,1)S(1)} %collective-permute-done), channel_id=1, source_target_pairs={{0,1},{1,2},{2,3},{3,0},{4,5},{5,6},{6,7},{7,4},{8,9},{9,10},{10,1... | collective-permute-start | bytes 786440 | tf_op jit(solution)/shard_map/ppermute | solution.py:14
  27.3 9.9 %collective-permute-start.2 = (bf16[64,2048]{1,0:T(8,128)(2,1)}, bf16[64,2048]{1,0:T(8,128)(2,1)}, u32[]{:S(2)}, u32[]{:S(2)}) collective-permute-start(bf16[64,2048]{1,0:T(8,128)(2,1)} %collective-permute-done.1), channel_id=1, source_target_pairs={{0,1},{1,2},{2,3},{3,0},{4,5},{5,6},{6,7},{7,4},{8,9},{9,10},{10,1... | collective-permute-start | bytes 786440 | tf_op jit(solution)/shard_map/ppermute | solution.py:14
  29.3 13.8 %copy-start.6 = (bf16[64,2048]{1,0:T(8,128)(2,1)S(1)}, bf16[64,2048]{1,0:T(8,128)(2,1)}, u32[]{:S(2)}) copy-start(bf16[64,2048]{1,0:T(8,128)(2,1)} %copy-done.5) | copy-start | bytes 786436
  30.0 14.5 %copy-start.8 = (bf16[256,64]{0,1:T(8,128)(2,1)S(1)}, bf16[256,64]{0,1:T(8,128)(2,1)}, u32[]{:S(2)}) copy-start(bf16[256,64]{0,1:T(8,128)(2,1)} %param.12) | copy-start | bytes 98308
  43.2 1.3 copy-start.2
  50.2 23.0 %copy-start.9 = (s32[96]{0:T(128)S(1)}, s32[96]{0:T(128)}, u32[]{:S(2)}) copy-start(s32[96]{0:T(128)} %param.16) | copy-start | bytes 1156
  50.2 73.2 %all-to-all-start = ((bf16[64,128,128]{2,0,1:T(8,128)(2,1)}), bf16[64,128,128]{2,0,1:T(8,128)(2,1)}, u32[]{:S(2)}, u32[]{:S(2)}) async-start(bf16[64,128,128]{2,0,1:T(8,128)(2,1)} %select_bitcast_fusion.1), calls=%async_computation | async-start | bytes 4194304 | tf_op jit(solution)/shard_map/all_to_all | solution.py:38
  80.8 51.9 %copy-start.12 = (bf16[64]{0:T(256)(128)(2,1)S(1)}, bf16[64]{0:T(256)(128)(2,1)}, u32[]{:S(2)}) copy-start(bf16[64]{0:T(256)(128)(2,1)} %param.13) | copy-start | bytes 388
  80.8 52.0 %copy-start.10 = (s32[96]{0:T(128)S(1)}, s32[96]{0:T(128)}, u32[]{:S(2)}) copy-start(s32[96]{0:T(128)} %param.15) | copy-start | bytes 1156
  123.4 105.8 %all-to-all-start.1 = ((bf16[128,128,128]{2,1,0:T(8,128)(2,1)}), bf16[128,128,128]{2,1,0:T(8,128)(2,1)}, u32[]{:S(2)}, u32[]{:S(2)}) async-start(bf16[128,128,128]{2,1,0:T(8,128)(2,1)} %copy.30), calls=%async_computation.1 | async-start | bytes 8388608 | tf_op jit(solution)/shard_map/all_to_all | solution.py:74
  143.4 3.3 copy-start.7
  229.2 73.6 %all-to-all-start.2 = ((bf16[64,128,128]{2,0,1:T(8,128)(2,1)}), bf16[64,128,128]{2,0,1:T(8,128)(2,1)}, u32[]{:S(2)}, u32[]{:S(2)}) async-start(bf16[64,128,128]{2,0,1:T(8,128)(2,1)} %select_bitcast_fusion), calls=%async_computation.2 | async-start | bytes 4194304 | tf_op jit(solution)/shard_map/all_to_all | solution.py:75
  252.0 325.0 %all-reduce.2.cloned.1.call-start = ((), (), s32[]{:S(2)}) async-start(), calls=%async_computation.4 | async-start | bytes 131072 | tf_op jit(solution)/shard_map/psum | solution.py:86
  258.4 48.6 %copy-start.11 = (s32[128]{0:T(128)S(1)}, s32[128]{0:T(128)}, u32[]{:S(2)}) copy-start(s32[128]{0:T(128)} %param.18) | copy-start | bytes 1540
  306.9 3.9 copy-start.1
  310.8 3.3 copy-start.3
  315.2 263.2 %all-gather.2.cloned.1.call-start = ((), (), s32[]{:S(2)}) async-start(), calls=%async_computation.3 | async-start | bytes 1310720 | tf_op jit(solution)/shard_map/all_gather | solution.py:91
Sparse Core Ops, SparseCore 0:
  315.3 174.1 all-reduce.1
Sparse Core Ops, SparseCore 1:
  318.4 20.8 all-gather.1
